TPU v7x, 512 devices: a whole 4x4x16 slice. The times are simulated.
512 devices in a mesh: seq: 128 (over x, z, core), head: 4 (over y).
Axes of the slice: x: 4, y: 4, z: 16, core: 2. Of those that a mesh axis runs over, the one named last changes fastest.
Arguments:
- hidden: bfloat16 [32768, 2560], P(('seq', 'head')), may hold values from -6 to 6
- w_values: bfloat16 [2560, 2560], P('seq', 'head'), may hold values from -0.125 to 0.125
- w_gates: bfloat16 [2560, 2560], P('seq', 'head'), may hold values from -0.125 to 0.125
- w_steps: bfloat16 [2560, 40], P('seq', 'head'), may hold values from -0.0625 to 0.0625
- w_states: bfloat16 [2560, 256], P('seq'), may hold values from -0.125 to 0.125
- conv_weight: float32 [4, 2816], replicated, may hold values from -3 to 3
- conv_bias: float32 [2816], replicated, may hold values from -3 to 3
- step_bias: float32 [40], P('head'), may hold values from -1 to 0.5
- decay_rate: float32 [40], P('head'), may hold values from 0 to 1, as said below
- skip_gain: float32 [40], P('head'), may hold values from 1 to 8
- norm_gain: float32 [2560], replicated, may hold values from 0.5 to 1.5
- lengths: int32 [64], replicated, may hold values from 256 to 768, as said below
Outputs:
- gated_out: bfloat16 [32768, 2560], P(('seq', 'head'))
- final_states: float32 [128, 40, 64, 128], P('seq', 'head')
Inputs may be any that keep to these rules, and one draw needn't show every extreme that they name: Prompts are packed in order, each holding 256 to 768 tokens; the lengths sum to 32768. `decay_rate`: positive rates.
All inputs are finite; a program needn't handle non-finite values.
Results may differ from a plain program's by a relative error of at most 0.01.
Values may be sent and summed in bfloat16 or wider, within the bound.
No kernel may reach another device: no remote copies, remote signals or barrier semaphores. Data moves between devices by JAX's collectives and lax.ppermute only.
A program may use at most 128 MiB of HBM per device.

v0:
```python
import jax
import jax.numpy as jnp
from jax import lax
from jax.sharding import Mesh, PartitionSpec as P

STRETCH = 256
SEQ = ("x", "z", "c")
epsilon = 1e-05


def from_behind(block, axis, distance):
    devices = range(lax.psum(1, axis))
    route = [(i - distance, i) for i in devices if i - distance in devices]
    return lax.ppermute(block, axis, route)


def segments_at(positions, prompt_ends):
    counted = jnp.sum((prompt_ends[None, :] <= positions[:, None]).astype(jnp.int32), axis=1)
    return jnp.where(positions < 0, -1, counted)


def on_device(
    hidden,
    w_values,
    w_gates,
    w_steps,
    w_states,
    conv_weight,
    conv_bias,
    step_bias,
    decay_rate,
    skip_gain,
    norm_gain,
    lengths,
):
    groups = lax.axis_size("head")
    group_index = lax.axis_index("head")
    block_index = lax.axis_index(SEQ)
    local_width = w_values.shape[1]
    inner_width = local_width * groups
    local_heads = decay_rate.shape[0]
    head_width = local_width // local_heads
    state_width = w_states.shape[1] // 2
    conv_taps = conv_weight.shape[0]
    prompt_ends = jnp.cumsum(lengths)
    block_hidden = lax.all_to_all(
        jnp.broadcast_to(hidden[None], (groups,) + hidden.shape), "head", 0, 0, tiled=True
    ).reshape(groups * hidden.shape[0], hidden.shape[1])
    block_rows = block_hidden.shape[0]
    sub_rows = block_rows // groups
    step_width = w_steps.shape[1]
    merged = jnp.concatenate([w_values, w_states, w_gates, w_steps], axis=1)
    shard_rows = merged.shape[0]
    padded_rows = -(-shard_rows // 16) * 16
    half = local_width + 2 * state_width
    merged = jnp.pad(merged, ((0, padded_rows - shard_rows), (0, 2 * half - merged.shape[1])))
    halves = jnp.stack([merged[:, :half], merged[:, half:]])
    own_half = lax.all_to_all(halves, "c", 0, 0, tiled=True).reshape(2 * padded_rows, half)
    own_half = lax.all_gather(own_half, "x", axis=0, tiled=True)
    early_start = block_index * block_rows
    ext_positions = (
        early_start - (conv_taps - 1) + jnp.arange(block_rows + conv_taps - 1, dtype=jnp.int32)
    )
    positions = early_start + jnp.arange(block_rows, dtype=jnp.int32)
    early_ids = (
        segments_at(ext_positions, prompt_ends),
        segments_at(positions, prompt_ends),
        segments_at(positions + 1, prompt_ends),
        segments_at(positions - 1, prompt_ends),
    )
    block_hidden, own_half, early_ids = lax.optimization_barrier(
        (block_hidden, own_half, early_ids)
    )
    ext_ids, segment_ids, next_ids, before_ids = early_ids
    own_half = lax.all_gather(own_half, "z", axis=0, tiled=True)
    other_half = lax.ppermute(own_half, "c", [(0, 1), (1, 0)])
    x_size = lax.psum(1, "x")
    z_size = lax.psum(1, "z")
    c_size = lax.psum(1, "c")
    core_index = lax.axis_index("c")

    def spread_rows(rows):
        count = rows.shape[0]
        split = rows.reshape(count, x_size, z_size, c_size, shard_rows)
        split = jnp.pad(split, ((0, 0), (0, 0), (0, 0), (0, 0), (0, padded_rows - shard_rows)))
        split = jnp.transpose(split, (0, 2, 1, 3, 4))
        return split.reshape(count, x_size * z_size * c_size * padded_rows)

    rim_hidden = from_behind(block_hidden[block_rows - (conv_taps - 1) :], SEQ, 1)
    rim_count = rim_hidden.shape[0]
    both_rows = jnp.concatenate(
        [block_hidden, rim_hidden, jnp.zeros((8 - rim_count, block_hidden.shape[1]), jnp.bfloat16)]
    )
    spread = spread_rows(both_rows)
    with_own = jnp.dot(spread, own_half, preferred_element_type=jnp.float32)
    with_other = jnp.dot(spread, other_half, preferred_element_type=jnp.float32)
    first_cols = jnp.where(core_index == 0, with_own, with_other)
    second_cols = jnp.where(core_index == 0, with_other, with_own)
    projected = jnp.concatenate([first_cols, second_cols], axis=1)
    conv_end = local_width + 2 * state_width
    prior_rim = projected[block_rows : block_rows + rim_count, :conv_end].astype(jnp.bfloat16)
    projected = projected[:block_rows]
    pre_rows = projected[:, :conv_end].astype(jnp.bfloat16)
    gates_sum = projected[:, conv_end : conv_end + local_width]
    steps_sum = projected[:, conv_end + local_width : conv_end + local_width + step_width]
    head_gates = gates_sum.astype(jnp.bfloat16)
    gates_tokens = lax.all_to_all(
        head_gates.reshape(groups, sub_rows, local_width), "head", 0, 2, tiled=True
    ).reshape(sub_rows, inner_width)
    local_taps = jnp.concatenate(
        [
            lax.dynamic_slice_in_dim(conv_weight, group_index * local_width, local_width, 1),
            conv_weight[:, inner_width:],
        ],
        axis=1,
    )
    local_bias = jnp.concatenate(
        [
            lax.dynamic_slice_in_dim(conv_bias, group_index * local_width, local_width, 0),
            conv_bias[inner_width:],
        ],
        axis=0,
    )
    block_start = block_index * block_rows
    extended = jnp.concatenate([prior_rim, pre_rows], axis=0)
    own_ids = ext_ids[conv_taps - 1 :]
    filtered = jnp.zeros(pre_rows.shape, jnp.float32) + local_bias[None, :]
    for offset in range(conv_taps):
        matches = (ext_ids[offset : offset + block_rows] == own_ids).astype(jnp.float32)
        filtered = (
            filtered
            + local_taps[offset][None, :]
            * extended[offset : offset + block_rows].astype(jnp.float32)
            * matches[:, None]
        )
    conv_out = jax.nn.silu(filtered).astype(jnp.bfloat16)
    head_values = conv_out[:, :local_width]
    both_states = conv_out[:, local_width:]
    stretch_rows = STRETCH
    stretches = block_rows // stretch_rows
    stretch_ids = segment_ids.reshape(stretches, stretch_rows)
    prior_ids = before_ids.reshape(stretches, stretch_rows)[:, 0]
    ends_mask = (segment_ids != next_ids).reshape(stretches, stretch_rows)
    step_sizes = jax.nn.softplus(steps_sum + step_bias[None, :])
    decay_steps = step_sizes * decay_rate[None, :]
    log_decay = -jnp.cumsum(decay_steps.reshape(stretches, stretch_rows, local_heads), axis=1)
    decay_heads = jnp.swapaxes(log_decay, 1, 2)
    step_heads = jnp.swapaxes(step_sizes.reshape(stretches, stretch_rows, local_heads), 1, 2)
    values = head_values.reshape(stretches, stretch_rows, local_heads, head_width)
    write_state = both_states[:, :state_width].reshape(stretches, stretch_rows, state_width)
    read_state = both_states[:, state_width:].reshape(stretches, stretch_rows, state_width)
    intersection = jnp.einsum(
        "ctn,csn->cts", read_state, write_state, preferred_element_type=jnp.float32
    )
    token_order = jnp.arange(stretch_rows, dtype=jnp.int32)
    causal = token_order[:, None] >= token_order[None, :]
    allowed = causal[None] & (stretch_ids[:, :, None] == stretch_ids[:, None, :])
    spread = decay_heads[:, :, :, None] - decay_heads[:, :, None, :]
    weights = (
        jnp.where(allowed[:, None], jnp.exp(jnp.minimum(spread, 0.0)), 0.0)
        * step_heads[:, :, None, :]
    )
    scores = (intersection[:, None] * weights).astype(jnp.bfloat16)
    within_stretch = jnp.einsum(
        "chts,cshp->cthp", scores, values, preferred_element_type=jnp.float32
    )
    last_ids = stretch_ids[:, -1]
    tail_decay = decay_heads[:, :, -1:]
    keep_tail = (stretch_ids == last_ids[:, None])[:, None, :]
    tail_coef = (
        jnp.where(keep_tail, jnp.exp(jnp.minimum(tail_decay - decay_heads, 0.0)), 0.0) * step_heads
    )
    tail_rows = (values.astype(jnp.float32) * jnp.swapaxes(tail_coef, 1, 2)[:, :, :, None]).astype(
        jnp.bfloat16
    )
    stretch_states = jnp.einsum(
        "clhp,cln->chpn", tail_rows, write_state, preferred_element_type=jnp.float32
    )
    stretch_gates = (
        jnp.exp(decay_heads[:, :, -1]) * (last_ids == prior_ids).astype(jnp.float32)[:, None]
    )
    own_gate = jnp.broadcast_to(stretch_gates[0][:, None, None], (local_heads, 8, state_width))
    packed = jnp.concatenate([stretch_states[0], own_gate], axis=1).astype(jnp.bfloat16)
    p1 = from_behind(packed, SEQ, 1)
    p2 = from_behind(packed, SEQ, 2)
    p3 = from_behind(packed, SEQ, 3)
    g1 = p1[:, head_width : head_width + 1, :1]
    g2 = p2[:, head_width : head_width + 1, :1]
    p1, p2, p3, g1, g2 = (part.astype(jnp.float32) for part in (p1, p2, p3, g1, g2))
    incoming = p1[:, :head_width] + g1 * (p2[:, :head_width] + g2 * p3[:, :head_width])
    arriving = incoming[None]
    carry_mask = (stretch_ids == prior_ids[:, None]).astype(jnp.float32)
    carry_decay = jnp.exp(log_decay) * carry_mask[:, :, None]
    from_before = (
        jnp.einsum(
            "cln,chpn->clhp",
            read_state,
            arriving.astype(jnp.bfloat16),
            preferred_element_type=jnp.float32,
        )
        * carry_decay[:, :, :, None]
    )
    result = (
        within_stretch + from_before + skip_gain[None, None, :, None] * values.astype(jnp.float32)
    )
    ssm_rows = result.reshape(block_rows, local_width).astype(jnp.bfloat16)
    end_weight = ends_mask.astype(jnp.float32)
    has_end = jnp.sum(end_weight, axis=1)
    end_decay = jnp.sum(decay_heads * end_weight[:, None, :], axis=2)
    end_ids = jnp.sum(jnp.where(ends_mask, stretch_ids, 0), axis=1)
    keep_end = ((stretch_ids == end_ids[:, None]) & (has_end[:, None] > 0))[:, None, :]
    end_coef = (
        jnp.where(keep_end, jnp.exp(jnp.minimum(end_decay[:, :, None] - decay_heads, 0.0)), 0.0)
        * step_heads
    )
    end_rows = (values.astype(jnp.float32) * jnp.swapaxes(end_coef, 1, 2)[:, :, :, None]).astype(
        jnp.bfloat16
    )
    end_states = jnp.einsum(
        "clhp,cln->chpn", end_rows, write_state, preferred_element_type=jnp.float32
    )
    end_carry = (
        jnp.exp(end_decay) * ((end_ids == prior_ids) & (has_end > 0)).astype(jnp.float32)[:, None]
    )
    end_states = end_states + end_carry[:, :, None, None] * arriving
    final_block = jnp.sum(end_states, axis=0)[None]
    y_tokens = lax.all_to_all(
        ssm_rows.reshape(groups, sub_rows, local_width), "head", 0, 2, tiled=True
    ).reshape(sub_rows, inner_width)
    token_rows = (y_tokens.astype(jnp.float32), gates_tokens.astype(jnp.float32))
    gated = token_rows[0] * jax.nn.silu(token_rows[1])
    mean_square = jnp.mean(gated * gated, axis=1)
    scaled = gated * lax.rsqrt(mean_square + epsilon)[:, None] * norm_gain[None, :]
    gated_out = scaled.astype(jnp.bfloat16)
    return (gated_out, final_block)


def solution(mesh):
    seq_size, head_size = mesh.devices.shape
    fine = Mesh(mesh.devices.reshape(4, seq_size // 8, 2, head_size), SEQ + ("head",))
    in_specs = (
        P(SEQ + ("head",), None),
        P(SEQ, "head"),
        P(SEQ, "head"),
        P(SEQ, "head"),
        P(SEQ, None),
        P(),
        P(),
        P("head"),
        P("head"),
        P("head"),
        P(),
        P(),
    )
    out_specs = (P(SEQ + ("head",), None), P(SEQ, "head", None, None))
    return jax.shard_map(
        on_device, mesh=fine, in_specs=in_specs, out_specs=out_specs, check_vma=False
    )
```

profile of v0, /device:TPU:1, one launch (start us, length us, event | category | flops | bytes accessed | tf_op | source)
XLA Modules:
  0.0 220.1 jit_solution(13898539905793476150)
XLA Ops:
  9.4 10.2 %all-to-all-start.1 = ((bf16[2,32,896]{2,1,0:T(8,128)(2,1)}), bf16[2,32,896]{2,1,0:T(8,128)(2,1)S(1)}, u32[]{:S(2)}, u32[]{:S(2)}) async-start(bf16[2,32,896]{2,1,0:T(8,128)(2,1)} %pad_maximum_fusion.2), calls=%async_computation.1 | async-start | bytes 229376 | tf_op jit(solution)/shard_map/all_to_all | solution.py:58
  20.8 2.1 broadcast_in_dim.39
  22.9 3.5 %all-to-all-start = ((bf16[4,64,2560]{2,1,0:T(8,128)(2,1)}), bf16[4,64,2560]{2,1,0:T(8,128)(2,1)S(1)}, u32[]{:S(2)}, u32[]{:S(2)}) async-start(bf16[4,64,2560]{2,1,0:T(8,128)(2,1)} %broadcast_in_dim.39), calls=%async_computation | async-start | bytes 2621440 | tf_op jit(solution)/shard_map/all_to_all | solution.py:46
  26.6 11.1 %all_gather.6 = bf16[256,896]{1,0:T(8,128)(2,1)} all-gather(bf16[64,896]{1,0:T(8,128)(2,1)S(1)} %bitcast.148), channel_id=1, replica_groups=mesh['x'=4,'z'=16,'c'=2,'head'=4] {'x'}, dimensions={0}, use_global_device_ids=true | all-gather | bytes 573440 | tf_op jit(solution)/shard_map/all_gather | solution.py:59
  37.7 6.4 %all-to-all-done = bf16[4,64,2560]{2,1,0:T(8,128)(2,1)S(1)} async-done(((bf16[4,64,2560]{2,1,0:T(8,128)(2,1)}), bf16[4,64,2560]{2,1,0:T(8,128)(2,1)S(1)}, u32[]{:S(2)}, u32[]{:S(2)}) %all-to-all-start) | async-done | bytes 1310752 | tf_op jit(solution)/shard_map/all_to_all | solution.py:46
  44.1 93.8 %all-gather.2.cloned.1.call-done = bf16[4096,896]{1,0:T(8,128)(2,1)} async-done(((bf16[256,896]{1,0:T(8,128)(2,1)}), bf16[4096,896]{1,0:T(8,128)(2,1)}) %all-gather.2.cloned.1.call-update) | async-done | bytes 7340048 | tf_op jit(solution)/shard_map/all_gather | solution.py:75
  137.9 2.6 %collective-permute-start.1 = (bf16[4096,896]{1,0:T(8,128)(2,1)}, bf16[4096,896]{1,0:T(8,128)(2,1)}, u32[]{:S(2)}, u32[]{:S(2)}) collective-permute-start(bf16[4096,896]{1,0:T(8,128)(2,1)} %all-gather.2.cloned.1.call-done), channel_id=1, source_target_pairs={{0,4},{4,0},{1,5},{5,1},{2,6},{6,2},{3,7},{7,3},{8,12},{12,8},{9,1... | collective-permute-start | bytes 22020104 | tf_op jit(solution)/shard_map/ppermute | solution.py:76
  142.2 1.9 collective-permute-start
  147.1 2.5 %broadcast_compare_fusion = (pred[256]{0:T(512)(128)(4,1)S(1)}, f32[256]{0:T(256)}, pred[256]{0:T(512)(128)(4,1)S(1)}) fusion(s32[256]{0:T(256)S(1)} %compare_select_fusion.3, s32[]{:T(128)} %bitcast.18, s32[]{:T(128)} %bitcast.29, pred[]{:T(512)} %gt.8, s32[]{:T(128)} %select_reduce_fusion), kind=kLoop, calls=%fused_computation.132 | loop fusion | flops 1280 | bytes 2573 | tf_op jit(solution)/shard_map/eq | solution.py:169
  152.7 2.4 %copy.131 = bf16[264,2560]{0,1:T(8,128)(2,1)} copy(bf16[264,2560]{1,0:T(8,128)(2,1)S(1)} %maximum_maximum_fusion) | data formatting | bytes 2703360 | tf_op jit(solution)/shard_map/concatenate | solution.py:91
  155.1 2.5 %reshape.411 = bf16[264,4,16,2,20]{0,4,3,2,1:T(8,128)(2,1)S(1)} reshape(bf16[264,2560]{0,1:T(8,128)(2,1)} %copy.131) | data formatting | bytes 2703360 | tf_op jit(solution)/shard_map/reshape | solution.py:84
  158.7 6.5 %fusion.65 = f32[264,896]{0,1:T(8,128)S(1)} fusion(bf16[264,4096]{0,1:T(8,128)(2,1)S(1)} %bitcast.140, bf16[4096,896]{1,0:T(8,128)(2,1)} %collective-permute-done.1), kind=kOutput, calls=%fused_computation.137 | convolution fusion | flops 1937768448 | bytes 10448896 | tf_op jit(solution)/shard_map/dot_general | solution.py:96
  165.3 4.0 %select_convert_fusion = (bf16[264,896]{0,1:T(8,128)(2,1)S(1)}, f32[264,896]{0,1:T(8,128)S(1)}) fusion(f32[264,896]{0,1:T(8,128)S(1)} %fusion.65, pred[]{:T(512)S(6)} %eq.70, bf16[264,4096]{0,1:T(8,128)(2,1)S(1)} %bitcast.141, bf16[4096,896]{1,0:T(8,128)(2,1)S(1)} %bitcast.162), kind=kOutput, calls=%fused_computation.2 | convolution fusion | flops 1938004992 | bytes 11868161 | tf_op jit(solution)/shard_map/dot_general | solution.py:95
  172.3 1.5 multiply_convert_fusion.4
  175.0 3.3 %collective-permute-start.3 = (bf16[10,72,128]{2,1,0:T(8,128)(2,1)}, bf16[10,72,128]{2,1,0:T(8,128)(2,1)}, u32[]{:S(2)}, u32[]{:S(2)}) collective-permute-start(bf16[10,72,128]{2,1,0:T(8,128)(2,1)} %pad_maximum_fusion.1), channel_id=1, source_target_pairs={{0,8},{4,12},{8,16},{12,20},{16,24},{20,28},{24,32},{28,36},{32,40... | collective-permute-start | bytes 552968 | tf_op jit(solution)/shard_map/ppermute | solution.py:14
  178.2 2.0 collective-permute-start.2
  180.3 4.9 %collective-permute-start.4 = (bf16[10,72,128]{2,1,0:T(8,128)(2,1)}, bf16[10,72,128]{2,1,0:T(8,128)(2,1)}, u32[]{:S(2)}, u32[]{:S(2)}) collective-permute-start(bf16[10,72,128]{2,1,0:T(8,128)(2,1)} %pad_maximum_fusion.1), channel_id=1, source_target_pairs={{0,12},{4,16},{8,20},{12,24},{16,28},{20,32},{24,36},{28,40},{32,4... | collective-permute-start | bytes 552968 | tf_op jit(solution)/shard_map/ppermute | solution.py:14
  187.8 4.0 %all-to-all-start.3 = ((bf16[4,64,640]{2,1,0:T(8,128)(2,1)}), bf16[4,64,640]{2,1,0:T(8,128)(2,1)S(1)}, u32[]{:S(2)}, u32[]{:S(2)}) async-start(bf16[4,64,640]{2,1,0:T(8,128)(2,1)} %bitcast.36), calls=%async_computation.3 | async-start | bytes 655360 | tf_op jit(solution)/shard_map/all_to_all | solution.py:107
  191.8 1.9 fusion.7
  195.5 1.4 fusion.11
  197.2 1.4 copy.144
  198.6 2.0 add_bitcast_fusion
  200.7 4.2 %all-to-all-start.2 = ((bf16[4,64,640]{2,1,0:T(8,128)(2,1)}), bf16[4,64,640]{2,1,0:T(8,128)(2,1)S(1)}, u32[]{:S(2)}, u32[]{:S(2)}) async-start(bf16[4,64,640]{2,1,0:T(8,128)(2,1)} %copy.144), calls=%async_computation.2 | async-start | bytes 655360 | tf_op jit(solution)/shard_map/all_to_all | solution.py:227
  205.4 6.0 %all-to-all-done.2 = bf16[4,64,640]{2,1,0:T(8,128)(2,1)S(1)} async-done(((bf16[4,64,640]{2,1,0:T(8,128)(2,1)}), bf16[4,64,640]{2,1,0:T(8,128)(2,1)S(1)}, u32[]{:S(2)}, u32[]{:S(2)}) %all-to-all-start.2) | async-done | bytes 327712 | tf_op jit(solution)/shard_map/all_to_all | solution.py:227
  (111 shorter events, 20.1 us)
Async XLA Ops:
  9.4 11.3 %all-to-all-start.1 = ((bf16[2,32,896]{2,1,0:T(8,128)(2,1)}), bf16[2,32,896]{2,1,0:T(8,128)(2,1)S(1)}, u32[]{:S(2)}, u32[]{:S(2)}) async-start(bf16[2,32,896]{2,1,0:T(8,128)(2,1)} %pad_maximum_fusion.2), calls=%async_computation.1 | async-start | bytes 229376 | tf_op jit(solution)/shard_map/all_to_all | solution.py:58
  20.7 121.3 %copy-start = (f32[4,2816]{1,0:T(4,128)S(1)}, f32[4,2816]{1,0:T(4,128)}, u32[]{:S(2)}) copy-start(f32[4,2816]{1,0:T(4,128)} %param.17) | copy-start | bytes 135172
  20.8 121.3 %slice-start = ((f32[4,2816]{1,0:T(4,128)}), f32[4,256]{1,0:T(4,128)S(1)}, s32[]{:S(2)}) async-start(f32[4,2816]{1,0:T(4,128)} %param.17), calls=%async_computation.5 | async-start | bytes 8192 | tf_op jit(solution)/shard_map/slice | solution.py:113
  22.9 21.2 %all-to-all-start = ((bf16[4,64,2560]{2,1,0:T(8,128)(2,1)}), bf16[4,64,2560]{2,1,0:T(8,128)(2,1)S(1)}, u32[]{:S(2)}, u32[]{:S(2)}) async-start(bf16[4,64,2560]{2,1,0:T(8,128)(2,1)} %broadcast_in_dim.39), calls=%async_computation | async-start | bytes 2621440 | tf_op jit(solution)/shard_map/all_to_all | solution.py:46
  26.5 111.5 %all-gather.2.cloned.1.call-start = ((), (), s32[]{:S(2)}) async-start(), calls=%async_computation.4 | async-start | bytes 7798784 | tf_op jit(solution)/shard_map/all_gather | solution.py:75
  137.9 20.8 %collective-permute-start.1 = (bf16[4096,896]{1,0:T(8,128)(2,1)}, bf16[4096,896]{1,0:T(8,128)(2,1)}, u32[]{:S(2)}, u32[]{:S(2)}) collective-permute-start(bf16[4096,896]{1,0:T(8,128)(2,1)} %all-gather.2.cloned.1.call-done), channel_id=1, source_target_pairs={{0,4},{4,0},{1,5},{5,1},{2,6},{6,2},{3,7},{7,3},{8,12},{12,8},{9,1... | collective-permute-start | bytes 22020104 | tf_op jit(solution)/shard_map/ppermute | solution.py:76
  142.2 10.2 %collective-permute-start = (bf16[3,2560]{1,0:T(4,128)(2,1)S(1)}, bf16[3,2560]{1,0:T(4,128)(2,1)S(1)}, u32[]{:S(2)}, u32[]{:S(2)}) collective-permute-start(bf16[3,2560]{1,0:T(4,128)(2,1)S(1)} %slice.128), channel_id=1, source_target_pairs={{0,4},{4,8},{8,12},{12,16},{16,20},{20,24},{24,28},{28,32},{32,36}... | collective-permute-start | bytes 46088 | tf_op jit(solution)/shard_map/ppermute | solution.py:14
  158.3 7.0 %slice-start.1 = ((s8[7340032]{0:T(1024)(128)(4,1)}), s8[4194304]{0:T(1024)(128)(4,1)S(1)}, s32[]{:S(2)}) async-start(s8[7340032]{0:T(1024)(128)(4,1)} %bitcast.161), calls=%async_computation.6 | async-start | bytes 8388608
  158.7 6.5 %slice-start.2 = ((s8[7340032]{0:T(1024)(128)(4,1)}), s8[3145728]{0:T(1024)(128)(4,1)S(1)}, s32[]{:S(2)}) async-start(s8[7340032]{0:T(1024)(128)(4,1)} %bitcast.161), calls=%async_computation.7 | async-start | bytes 6291456
  169.3 0.7 copy-start.2
  169.3 0.7 copy-start.5
  171.8 13.4 %copy-start.4 = (f32[10]{0:T(128)}, f32[10]{0:T(128)S(1)}, u32[]{:S(2)}) copy-start(f32[10]{0:T(128)S(1)} %multiply_reduce_fusion.1) | copy-start | bytes 124
  175.0 18.8 %collective-permute-start.3 = (bf16[10,72,128]{2,1,0:T(8,128)(2,1)}, bf16[10,72,128]{2,1,0:T(8,128)(2,1)}, u32[]{:S(2)}, u32[]{:S(2)}) collective-permute-start(bf16[10,72,128]{2,1,0:T(8,128)(2,1)} %pad_maximum_fusion.1), channel_id=1, source_target_pairs={{0,8},{4,12},{8,16},{12,20},{16,24},{20,28},{24,32},{28,36},{32,40... | collective-permute-start | bytes 552968 | tf_op jit(solution)/shard_map/ppermute | solution.py:14
  178.2 16.4 %collective-permute-start.2 = (bf16[10,72,128]{2,1,0:T(8,128)(2,1)}, bf16[10,72,128]{2,1,0:T(8,128)(2,1)}, u32[]{:S(2)}, u32[]{:S(2)}) collective-permute-start(bf16[10,72,128]{2,1,0:T(8,128)(2,1)} %pad_maximum_fusion.1), channel_id=1, source_target_pairs={{0,4},{4,8},{8,12},{12,16},{16,20},{20,24},{24,28},{28,32},{32,36}... | collective-permute-start | bytes 552968 | tf_op jit(solution)/shard_map/ppermute | solution.py:14
  180.3 15.3 %collective-permute-start.4 = (bf16[10,72,128]{2,1,0:T(8,128)(2,1)}, bf16[10,72,128]{2,1,0:T(8,128)(2,1)}, u32[]{:S(2)}, u32[]{:S(2)}) collective-permute-start(bf16[10,72,128]{2,1,0:T(8,128)(2,1)} %pad_maximum_fusion.1), channel_id=1, source_target_pairs={{0,12},{4,16},{8,20},{12,24},{16,28},{20,32},{24,36},{28,40},{32,4... | collective-permute-start | bytes 552968 | tf_op jit(solution)/shard_map/ppermute | solution.py:14
  187.8 12.9 %all-to-all-start.3 = ((bf16[4,64,640]{2,1,0:T(8,128)(2,1)}), bf16[4,64,640]{2,1,0:T(8,128)(2,1)S(1)}, u32[]{:S(2)}, u32[]{:S(2)}) async-start(bf16[4,64,640]{2,1,0:T(8,128)(2,1)} %bitcast.36), calls=%async_computation.3 | async-start | bytes 655360 | tf_op jit(solution)/shard_map/all_to_all | solution.py:107
  191.8 1.9 copy-start.3
  191.8 3.7 %copy-start.6 = (f32[10]{0:T(128)S(1)}, f32[10]{0:T(128)}, u32[]{:S(2)}) copy-start(f32[10]{0:T(128)} %param.21) | copy-start | bytes 124
  200.7 10.8 %all-to-all-start.2 = ((bf16[4,64,640]{2,1,0:T(8,128)(2,1)}), bf16[4,64,640]{2,1,0:T(8,128)(2,1)S(1)}, u32[]{:S(2)}, u32[]{:S(2)}) async-start(bf16[4,64,640]{2,1,0:T(8,128)(2,1)} %copy.144), calls=%async_computation.2 | async-start | bytes 655360 | tf_op jit(solution)/shard_map/all_to_all | solution.py:227
  205.4 6.9 %copy-start.1 = (f32[2560]{0:T(1024)S(1)}, f32[2560]{0:T(1024)}, u32[]{:S(2)}) copy-start(f32[2560]{0:T(1024)} %param.22) | copy-start | bytes 30724
Sparse Core Ops, SparseCore 0:
  44.2 93.6 all-gather.1
where the time goes:
time: 221 us; the launch traced here: 220 us
  waiting for transfers between devices  106 us (48%)
  starting transfers between devices  36.7 us (17%)
  between operations  17.7 us (8%)
  local copies, waits for them, and re-layouts  17.1 us (8%)
  matrix products  17 us (8%)
  other arithmetic  14.2 us (6%)
  blocking collectives  11.1 us (5%)
    all_gather x1, waiting for transfers between devices, on_device(): own_half = lax.all_gather(own_half, 'z', axis=0, tiled=True)  93.8 us
    ppermute x4, starting transfers between devices, from_behind(): return lax.ppermute(block, axis, route)  12.1 us
    all_gather x1, blocking collectives, on_device(): own_half = lax.all_gather(own_half, 'x', axis=0, tiled=True)  11.1 us
    all_to_all x1, starting transfers between devices, on_device(): lax.all_to_all(halves, 'c', 0, 0, tiled=True).reshape(2 * padded_rows, half)  10.2 us
    dot_general x1, matrix products, on_device(): with_other = jnp.dot(spread, other_half, preferred_element_type=jnp.float32)  6.52 us
    all_to_all x1, waiting for transfers between devices, on_device(): lax.all_to_all(jnp.broadcast_to(hidden[None], (groups,) + hidden.shape),...  6.39 us
    all_to_all x1, waiting for transfers between devices, on_device(): lax.all_to_all(ssm_rows.reshape(groups, sub_rows, local_width), 'head', 0...  5.98 us
  transfers between devices with their start and end apart: 10, of which 3 were waited for; matrix products, arithmetic and copies ran while one was open for 12% of the time, Pallas kernels for 0%

commit v1 on v0

--- a/solution.py
+++ b/solution.py
@@ -224,8 +224,18 @@
     )
     end_states = end_states + end_carry[:, :, None, None] * arriving
     final_block = jnp.sum(end_states, axis=0)[None]
-    y_tokens = lax.all_to_all(
-        ssm_rows.reshape(groups, sub_rows, local_width), "head", 0, 2, tiled=True
+    y_tokens = jnp.concatenate(
+        lax.all_to_all(
+            jnp.stack(
+                jnp.split(
+                    ssm_rows.reshape(groups, sub_rows, local_width), lax.axis_size("head"), axis=0
+                )
+            ),
+            "head",
+            0,
+            0,
+        ),
+        axis=2,
     ).reshape(sub_rows, inner_width)
     token_rows = (y_tokens.astype(jnp.float32), gates_tokens.astype(jnp.float32))
     gated = token_rows[0] * jax.nn.silu(token_rows[1])

time: 221 us -> 221 us (level)
  no operation moved by 1% of the time
where the time goes in v1:
time: 221 us; the launch traced here: 220 us
  waiting for transfers between devices  106 us (48%)
  starting transfers between devices  36.7 us (17%)
  between operations  17.7 us (8%)
  matrix products  17 us (8%)
  local copies, waits for them, and re-layouts  16.2 us (7%)
  other arithmetic  15 us (7%)
  blocking collectives  11.1 us (5%)
    all_gather x1, waiting for transfers between devices, on_device(): own_half = lax.all_gather(own_half, 'z', axis=0, tiled=True)  93.8 us
    ppermute x4, starting transfers between devices, from_behind(): return lax.ppermute(block, axis, route)  12.1 us
    all_gather x1, blocking collectives, on_device(): own_half = lax.all_gather(own_half, 'x', axis=0, tiled=True)  11.1 us
    all_to_all x1, starting transfers between devices, on_device(): lax.all_to_all(halves, 'c', 0, 0, tiled=True).reshape(2 * padded_rows, half)  10.2 us
    dot_general x1, matrix products, on_device(): with_other = jnp.dot(spread, other_half, preferred_element_type=jnp.float32)  6.52 us
    all_to_all x1, waiting for transfers between devices, on_device(): lax.all_to_all(jnp.broadcast_to(hidden[None], (groups,) + hidden.shape),...  6.39 us
    all_to_all x1, waiting for transfers between devices, on_device(): lax.all_to_all(jnp.stack(jnp.split(ssm_rows.reshape(groups, sub_rows, loc...  5.99 us
  transfers between devices with their start and end apart: 10, of which 3 were waited for; matrix products, arithmetic and copies ran while one was open for 12% of the time, Pallas kernels for 0%

profile of v1, /device:TPU:1, one launch (start us, length us, event | category | flops | bytes accessed | tf_op | source)
XLA Modules:
  0.0 220.0 jit_solution(18335017534258997284)
XLA Ops:
  9.4 10.2 %all-to-all-start.1 = ((bf16[2,32,896]{2,1,0:T(8,128)(2,1)}), bf16[2,32,896]{2,1,0:T(8,128)(2,1)S(1)}, u32[]{:S(2)}, u32[]{:S(2)}) async-start(bf16[2,32,896]{2,1,0:T(8,128)(2,1)} %pad_maximum_fusion.3), calls=%async_computation.1 | async-start | bytes 229376 | tf_op jit(solution)/shard_map/all_to_all | solution.py:58
  20.8 2.1 broadcast_in_dim.39
  22.9 3.5 %all-to-all-start = ((bf16[4,64,2560]{2,1,0:T(8,128)(2,1)}), bf16[4,64,2560]{2,1,0:T(8,128)(2,1)S(1)}, u32[]{:S(2)}, u32[]{:S(2)}) async-start(bf16[4,64,2560]{2,1,0:T(8,128)(2,1)} %broadcast_in_dim.39), calls=%async_computation | async-start | bytes 2621440 | tf_op jit(solution)/shard_map/all_to_all | solution.py:46
  26.6 11.1 %all_gather.6 = bf16[256,896]{1,0:T(8,128)(2,1)} all-gather(bf16[64,896]{1,0:T(8,128)(2,1)S(1)} %bitcast.151), channel_id=1, replica_groups=mesh['x'=4,'z'=16,'c'=2,'head'=4] {'x'}, dimensions={0}, use_global_device_ids=true | all-gather | bytes 573440 | tf_op jit(solution)/shard_map/all_gather | solution.py:59
  37.7 6.4 %all-to-all-done = bf16[4,64,2560]{2,1,0:T(8,128)(2,1)S(1)} async-done(((bf16[4,64,2560]{2,1,0:T(8,128)(2,1)}), bf16[4,64,2560]{2,1,0:T(8,128)(2,1)S(1)}, u32[]{:S(2)}, u32[]{:S(2)}) %all-to-all-start) | async-done | bytes 1310752 | tf_op jit(solution)/shard_map/all_to_all | solution.py:46
  44.1 93.8 %all-gather.2.cloned.1.call-done = bf16[4096,896]{1,0:T(8,128)(2,1)} async-done(((bf16[256,896]{1,0:T(8,128)(2,1)}), bf16[4096,896]{1,0:T(8,128)(2,1)}) %all-gather.2.cloned.1.call-update) | async-done | bytes 7340048 | tf_op jit(solution)/shard_map/all_gather | solution.py:75
  137.9 2.6 %collective-permute-start.1 = (bf16[4096,896]{1,0:T(8,128)(2,1)}, bf16[4096,896]{1,0:T(8,128)(2,1)}, u32[]{:S(2)}, u32[]{:S(2)}) collective-permute-start(bf16[4096,896]{1,0:T(8,128)(2,1)} %all-gather.2.cloned.1.call-done), channel_id=1, source_target_pairs={{0,4},{4,0},{1,5},{5,1},{2,6},{6,2},{3,7},{7,3},{8,12},{12,8},{9,1... | collective-permute-start | bytes 22020104 | tf_op jit(solution)/shard_map/ppermute | solution.py:76
  142.2 1.9 collective-permute-start
  147.1 2.5 %broadcast_compare_fusion = (pred[256]{0:T(512)(128)(4,1)S(1)}, f32[256]{0:T(256)}, pred[256]{0:T(512)(128)(4,1)S(1)}) fusion(s32[256]{0:T(256)S(1)} %compare_select_fusion.3, s32[]{:T(128)} %bitcast.18, s32[]{:T(128)} %bitcast.29, pred[]{:T(512)} %gt.8, s32[]{:T(128)} %select_reduce_fusion), kind=kLoop, calls=%fused_computation.133 | loop fusion | flops 1280 | bytes 2573 | tf_op jit(solution)/shard_map/eq | solution.py:169
  152.7 2.4 %copy.173 = bf16[264,2560]{0,1:T(8,128)(2,1)} copy(bf16[264,2560]{1,0:T(8,128)(2,1)S(1)} %maximum_maximum_fusion) | data formatting | bytes 2703360 | tf_op jit(solution)/shard_map/concatenate | solution.py:91
  155.1 2.5 %reshape.421 = bf16[264,4,16,2,20]{0,4,3,2,1:T(8,128)(2,1)S(1)} reshape(bf16[264,2560]{0,1:T(8,128)(2,1)} %copy.173) | data formatting | bytes 2703360 | tf_op jit(solution)/shard_map/reshape | solution.py:84
  158.7 6.5 %fusion.66 = f32[264,896]{0,1:T(8,128)S(1)} fusion(bf16[264,4096]{0,1:T(8,128)(2,1)S(1)} %bitcast.139, bf16[4096,896]{1,0:T(8,128)(2,1)} %collective-permute-done.1), kind=kOutput, calls=%fused_computation.139 | convolution fusion | flops 1937768448 | bytes 10448896 | tf_op jit(solution)/shard_map/dot_general | solution.py:96
  165.3 4.0 %select_convert_fusion = (bf16[264,896]{0,1:T(8,128)(2,1)S(1)}, f32[264,896]{0,1:T(8,128)S(1)}) fusion(f32[264,896]{0,1:T(8,128)S(1)} %fusion.66, pred[]{:T(512)S(6)} %eq.70, bf16[264,4096]{0,1:T(8,128)(2,1)S(1)} %bitcast.140, bf16[4096,896]{1,0:T(8,128)(2,1)S(1)} %bitcast.165), kind=kOutput, calls=%fused_computation.2 | convolution fusion | flops 1938004992 | bytes 11868161 | tf_op jit(solution)/shard_map/dot_general | solution.py:95
  172.3 1.5 multiply_convert_fusion.4
  175.0 3.3 %collective-permute-start.3 = (bf16[10,72,128]{2,1,0:T(8,128)(2,1)}, bf16[10,72,128]{2,1,0:T(8,128)(2,1)}, u32[]{:S(2)}, u32[]{:S(2)}) collective-permute-start(bf16[10,72,128]{2,1,0:T(8,128)(2,1)} %pad_maximum_fusion.2), channel_id=1, source_target_pairs={{0,8},{4,12},{8,16},{12,20},{16,24},{20,28},{24,32},{28,36},{32,40... | collective-permute-start | bytes 552968 | tf_op jit(solution)/shard_map/ppermute | solution.py:14
  178.2 2.0 collective-permute-start.2
  180.3 4.9 %collective-permute-start.4 = (bf16[10,72,128]{2,1,0:T(8,128)(2,1)}, bf16[10,72,128]{2,1,0:T(8,128)(2,1)}, u32[]{:S(2)}, u32[]{:S(2)}) collective-permute-start(bf16[10,72,128]{2,1,0:T(8,128)(2,1)} %pad_maximum_fusion.2), channel_id=1, source_target_pairs={{0,12},{4,16},{8,20},{12,24},{16,28},{20,32},{24,36},{28,40},{32,4... | collective-permute-start | bytes 552968 | tf_op jit(solution)/shard_map/ppermute | solution.py:14
  187.8 4.0 %all-to-all-start.3 = ((bf16[4,64,640]{2,1,0:T(8,128)(2,1)}), bf16[4,64,640]{2,1,0:T(8,128)(2,1)S(1)}, u32[]{:S(2)}, u32[]{:S(2)}) async-start(bf16[4,64,640]{2,1,0:T(8,128)(2,1)} %bitcast.40), calls=%async_computation.3 | async-start | bytes 655360 | tf_op jit(solution)/shard_map/all_to_all | solution.py:107
  191.8 1.9 fusion.7
  195.5 1.4 fusion.11
  198.5 2.0 add_bitcast_fusion
  200.6 4.2 %all-to-all-start.2 = ((bf16[4,1,64,640]{3,2,1,0:T(8,128)(2,1)}), bf16[4,1,64,640]{3,2,1,0:T(8,128)(2,1)S(1)}, u32[]{:S(2)}, u32[]{:S(2)}) async-start(bf16[4,1,64,640]{3,2,1,0:T(8,128)(2,1)} %pad_maximum_fusion.1), calls=%async_computation.2 | async-start | bytes 655360 | tf_op jit(solution)/shard_map/all_to_all | solution.py:228
  205.3 6.0 %all-to-all-done.2 = bf16[4,1,64,640]{3,2,1,0:T(8,128)(2,1)S(1)} async-done(((bf16[4,1,64,640]{3,2,1,0:T(8,128)(2,1)}), bf16[4,1,64,640]{3,2,1,0:T(8,128)(2,1)S(1)}, u32[]{:S(2)}, u32[]{:S(2)}) %all-to-all-start.2) | async-done | bytes 327712 | tf_op jit(solution)/shard_map/all_to_all | solution.py:228
  212.2 1.0 multiply_convert_fusion.5
  (115 shorter events, 20.5 us)
Async XLA Ops:
  9.4 11.3 %all-to-all-start.1 = ((bf16[2,32,896]{2,1,0:T(8,128)(2,1)}), bf16[2,32,896]{2,1,0:T(8,128)(2,1)S(1)}, u32[]{:S(2)}, u32[]{:S(2)}) async-start(bf16[2,32,896]{2,1,0:T(8,128)(2,1)} %pad_maximum_fusion.3), calls=%async_computation.1 | async-start | bytes 229376 | tf_op jit(solution)/shard_map/all_to_all | solution.py:58
  20.7 121.3 %copy-start = (f32[4,2816]{1,0:T(4,128)S(1)}, f32[4,2816]{1,0:T(4,128)}, u32[]{:S(2)}) copy-start(f32[4,2816]{1,0:T(4,128)} %param.17) | copy-start | bytes 135172
  20.8 121.3 %slice-start = ((f32[4,2816]{1,0:T(4,128)}), f32[4,256]{1,0:T(4,128)S(1)}, s32[]{:S(2)}) async-start(f32[4,2816]{1,0:T(4,128)} %param.17), calls=%async_computation.5 | async-start | bytes 8192 | tf_op jit(solution)/shard_map/slice | solution.py:113
  22.9 21.2 %all-to-all-start = ((bf16[4,64,2560]{2,1,0:T(8,128)(2,1)}), bf16[4,64,2560]{2,1,0:T(8,128)(2,1)S(1)}, u32[]{:S(2)}, u32[]{:S(2)}) async-start(bf16[4,64,2560]{2,1,0:T(8,128)(2,1)} %broadcast_in_dim.39), calls=%async_computation | async-start | bytes 2621440 | tf_op jit(solution)/shard_map/all_to_all | solution.py:46
  26.5 111.5 %all-gather.2.cloned.1.call-start = ((), (), s32[]{:S(2)}) async-start(), calls=%async_computation.4 | async-start | bytes 7798784 | tf_op jit(solution)/shard_map/all_gather | solution.py:75
  137.9 20.8 %collective-permute-start.1 = (bf16[4096,896]{1,0:T(8,128)(2,1)}, bf16[4096,896]{1,0:T(8,128)(2,1)}, u32[]{:S(2)}, u32[]{:S(2)}) collective-permute-start(bf16[4096,896]{1,0:T(8,128)(2,1)} %all-gather.2.cloned.1.call-done), channel_id=1, source_target_pairs={{0,4},{4,0},{1,5},{5,1},{2,6},{6,2},{3,7},{7,3},{8,12},{12,8},{9,1... | collective-permute-start | bytes 22020104 | tf_op jit(solution)/shard_map/ppermute | solution.py:76
  142.2 10.2 %collective-permute-start = (bf16[3,2560]{1,0:T(4,128)(2,1)S(1)}, bf16[3,2560]{1,0:T(4,128)(2,1)S(1)}, u32[]{:S(2)}, u32[]{:S(2)}) collective-permute-start(bf16[3,2560]{1,0:T(4,128)(2,1)S(1)} %slice.136), channel_id=1, source_target_pairs={{0,4},{4,8},{8,12},{12,16},{16,20},{20,24},{24,28},{28,32},{32,36}... | collective-permute-start | bytes 46088 | tf_op jit(solution)/shard_map/ppermute | solution.py:14
  158.3 7.0 %slice-start.1 = ((s8[7340032]{0:T(1024)(128)(4,1)}), s8[4194304]{0:T(1024)(128)(4,1)S(1)}, s32[]{:S(2)}) async-start(s8[7340032]{0:T(1024)(128)(4,1)} %bitcast.164), calls=%async_computation.6 | async-start | bytes 8388608
  158.7 6.5 %slice-start.2 = ((s8[7340032]{0:T(1024)(128)(4,1)}), s8[3145728]{0:T(1024)(128)(4,1)S(1)}, s32[]{:S(2)}) async-start(s8[7340032]{0:T(1024)(128)(4,1)} %bitcast.164), calls=%async_computation.7 | async-start | bytes 6291456
  169.3 0.7 copy-start.2
  169.3 0.7 copy-start.5
  171.8 13.4 %copy-start.4 = (f32[10]{0:T(128)}, f32[10]{0:T(128)S(1)}, u32[]{:S(2)}) copy-start(f32[10]{0:T(128)S(1)} %multiply_reduce_fusion.1) | copy-start | bytes 124
  175.0 18.8 %collective-permute-start.3 = (bf16[10,72,128]{2,1,0:T(8,128)(2,1)}, bf16[10,72,128]{2,1,0:T(8,128)(2,1)}, u32[]{:S(2)}, u32[]{:S(2)}) collective-permute-start(bf16[10,72,128]{2,1,0:T(8,128)(2,1)} %pad_maximum_fusion.2), channel_id=1, source_target_pairs={{0,8},{4,12},{8,16},{12,20},{16,24},{20,28},{24,32},{28,36},{32,40... | collective-permute-start | bytes 552968 | tf_op jit(solution)/shard_map/ppermute | solution.py:14
  178.2 16.4 %collective-permute-start.2 = (bf16[10,72,128]{2,1,0:T(8,128)(2,1)}, bf16[10,72,128]{2,1,0:T(8,128)(2,1)}, u32[]{:S(2)}, u32[]{:S(2)}) collective-permute-start(bf16[10,72,128]{2,1,0:T(8,128)(2,1)} %pad_maximum_fusion.2), channel_id=1, source_target_pairs={{0,4},{4,8},{8,12},{12,16},{16,20},{20,24},{24,28},{28,32},{32,36}... | collective-permute-start | bytes 552968 | tf_op jit(solution)/shard_map/ppermute | solution.py:14
  180.3 15.3 %collective-permute-start.4 = (bf16[10,72,128]{2,1,0:T(8,128)(2,1)}, bf16[10,72,128]{2,1,0:T(8,128)(2,1)}, u32[]{:S(2)}, u32[]{:S(2)}) collective-permute-start(bf16[10,72,128]{2,1,0:T(8,128)(2,1)} %pad_maximum_fusion.2), channel_id=1, source_target_pairs={{0,12},{4,16},{8,20},{12,24},{16,28},{20,32},{24,36},{28,40},{32,4... | collective-permute-start | bytes 552968 | tf_op jit(solution)/shard_map/ppermute | solution.py:14
  187.8 12.7 %all-to-all-start.3 = ((bf16[4,64,640]{2,1,0:T(8,128)(2,1)}), bf16[4,64,640]{2,1,0:T(8,128)(2,1)S(1)}, u32[]{:S(2)}, u32[]{:S(2)}) async-start(bf16[4,64,640]{2,1,0:T(8,128)(2,1)} %bitcast.40), calls=%async_computation.3 | async-start | bytes 655360 | tf_op jit(solution)/shard_map/all_to_all | solution.py:107
  191.8 1.9 copy-start.3
  191.8 3.7 %copy-start.6 = (f32[10]{0:T(128)S(1)}, f32[10]{0:T(128)}, u32[]{:S(2)}) copy-start(f32[10]{0:T(128)} %param.21) | copy-start | bytes 124
  200.6 10.8 %all-to-all-start.2 = ((bf16[4,1,64,640]{3,2,1,0:T(8,128)(2,1)}), bf16[4,1,64,640]{3,2,1,0:T(8,128)(2,1)S(1)}, u32[]{:S(2)}, u32[]{:S(2)}) async-start(bf16[4,1,64,640]{3,2,1,0:T(8,128)(2,1)} %pad_maximum_fusion.1), calls=%async_computation.2 | async-start | bytes 655360 | tf_op jit(solution)/shard_map/all_to_all | solution.py:228
  205.3 6.9 %copy-start.1 = (f32[2560]{0:T(1024)S(1)}, f32[2560]{0:T(1024)}, u32[]{:S(2)}) copy-start(f32[2560]{0:T(1024)} %param.22) | copy-start | bytes 30724
Sparse Core Ops, SparseCore 0:
  44.2 93.6 all-gather.1
